TPU v7x, 128 devices: a whole 4x4x4 slice. The times are simulated.
128 devices in a mesh: dof: 32 (over x, z, core), snap: 4 (over y).
Axes of the slice: x: 4, y: 4, z: 4, core: 2. Of those that a mesh axis runs over, the one named last changes fastest.
Arguments:
- snapshots: bfloat16 [131072, 1024], P('dof', 'snap')
- lengths: int32 [16], replicated, may hold values from 16 to 64, as said below
- start_block: float32 [1024, 128], replicated, may hold values from -6 to 6
Outputs:
- pod_modes: float32 [131072, 128], P(('dof', 'snap'))
- r_factor: float32 [1024, 1024], replicated
Inputs may be any that keep to these rules, and one draw needn't show every extreme that they name: `lengths`: some passage has all 64 steps active and some passage only a quarter of them.
All inputs are finite; a program needn't handle non-finite values.
Results may differ from a plain program's by a relative error of at most 0.0003.
Values may be sent and summed in bfloat16 or wider, within the bound.
No kernel may reach another device: no remote copies, remote signals or barrier semaphores. Data moves between devices by JAX's collectives and lax.ppermute only.
A program may use at most 128 MiB of HBM per device.

v0:
```python
import jax
import jax.numpy as jnp
from jax import lax
from jax.sharding import PartitionSpec as P

STEPS = 64
ITERS = 3
PASSES = 16


def body(snapshots, lengths, start_block):
    panel_width = snapshots.shape[1]
    first_col = lax.axis_index("snap") * panel_width
    columns = first_col + jnp.arange(panel_width, dtype=jnp.int32)
    passage = columns // STEPS
    lookup = passage[:, None] == jnp.arange(PASSES, dtype=jnp.int32)[None, :]
    col_length = jnp.sum(jnp.where(lookup, lengths[None, :], 0), axis=1)
    active = columns % STEPS < col_length
    masked = jnp.where(active[None, :], snapshots, jnp.zeros_like(snapshots))
    gathered_slab = lax.all_gather(masked, "snap", axis=1, tiled=True)
    row_count = gathered_slab.shape[0] * lax.axis_size("dof")
    contract = (((0,), (0,)), ((), ()))
    partial_gram = lax.dot_general(
        gathered_slab, gathered_slab, contract, preferred_element_type=jnp.float32
    )
    gram_sum = lax.psum(partial_gram, "dof")
    width = gram_sum.shape[0]
    shifted = gram_sum / jnp.float32(row_count) + 0.05 * jnp.eye(width, dtype=jnp.float32)
    upper_factor = jnp.linalg.cholesky(shifted).T
    subspace = start_block
    for sweep in range(ITERS):
        image = jnp.dot(
            shifted, subspace, precision=lax.Precision.HIGHEST, preferred_element_type=jnp.float32
        )
        correlation = lax.dot_general(
            image,
            image,
            contract,
            precision=lax.Precision.HIGHEST,
            preferred_element_type=jnp.float32,
        )
        lower_factor = jnp.linalg.cholesky(correlation)
        subspace = lax.linalg.triangular_solve(
            lower_factor, image, left_side=False, lower=True, transpose_a=True
        )
    quarter = gathered_slab.shape[0] // lax.axis_size("snap")
    own_rows = lax.dynamic_slice_in_dim(
        gathered_slab, lax.axis_index("snap") * quarter, quarter, 0
    ).astype(jnp.float32)
    pod_modes = jnp.dot(
        own_rows, subspace, precision=lax.Precision.HIGHEST, preferred_element_type=jnp.float32
    )
    return (pod_modes, upper_factor)


def solution(mesh):
    placed = (P("dof", "snap"), P(), P())
    return jax.shard_map(
        body, mesh=mesh, in_specs=placed, out_specs=(P(("dof", "snap"), None), P()), check_vma=False
    )
```

profile of v0, /device:TPU:1, one launch (start us, length us, event | category | flops | bytes accessed | tf_op | source)
XLA Modules:
  0.0 570.0 jit_solution(12406197987237153935)
XLA Ops:
  11.2 89.9 %all-gather.2.cloned.1.call-done = bf16[4096,1024]{1,0:T(8,128)(2,1)} async-done(((bf16[4096,256]{1,0:T(8,128)(2,1)}), bf16[4096,1024]{1,0:T(8,128)(2,1)}) %all-gather.2.cloned.1.call-update) | async-done | bytes 8388624 | tf_op jit(solution)/shard_map/all_gather | solution.py:20
  101.0 15.0 %fusion.79 = f32[1024,1024]{0,1:T(8,128)} fusion(bf16[4096,1024]{1,0:T(8,128)(2,1)} %all-gather.2.cloned.1.call-done), kind=kOutput, calls=%fused_computation.138 | convolution fusion | flops 8589934592 | bytes 12582912 | tf_op jit(solution)/shard_map/dot_general | solution.py:23
  116.1 113.1 %all-reduce.3.cloned.1.call-done = f32[1024,1024]{0,1:T(8,128)} async-done(((f32[1024,1024]{0,1:T(8,128)}), f32[1024,1024]{0,1:T(8,128)}) %all-reduce.3.cloned.1.call-update) | async-done | bytes 4194320 | tf_op jit(solution)/shard_map/psum | solution.py:26
  229.2 5.1 select_add_fusion
  234.3 5.8 %copy.29 = f32[1024,1024]{1,0:T(8,128)} copy(f32[1024,1024]{0,1:T(8,128)} %select_add_fusion) | data formatting | bytes 8388608 | tf_op jit(solution)/shard_map/add | solution.py:28
  240.1 4.5 fusion
  246.6 11.7 %cholesky.247 = f32[128,128]{1,0:T(8,128)S(1)} custom-call(f32[128,128]{1,0:T(8,128)S(1)} %cholesky.667), custom_call_target="Cholesky" | custom-call | tf_op jit(solution)/shard_map/jit(cholesky)/cholesky | solution.py:29
  258.5 9.8 %custom-call.64 = f32[1,128,128]{1,2,0:T(8,128)S(1)} custom-call(f32[1,128,128]{2,1,0:T(8,128)S(1)} %get-tuple-element.17), custom_call_target="InvertDiagBlocksLowerTriangular" | custom-call | tf_op jit(solution)/shard_map/jit(cholesky)/cholesky | solution.py:29
  271.6 11.7 %cholesky.270 = f32[128,128]{1,0:T(8,128)S(1)} custom-call(f32[128,128]{1,0:T(8,128)S(1)} %cholesky.671), custom_call_target="Cholesky" | custom-call | tf_op jit(solution)/shard_map/jit(cholesky)/cholesky | solution.py:29
  283.6 9.8 %custom-call.65 = f32[1,128,128]{1,2,0:T(8,128)S(1)} custom-call(f32[1,128,128]{2,1,0:T(8,128)S(1)} %get-tuple-element.15), custom_call_target="InvertDiagBlocksLowerTriangular" | custom-call | tf_op jit(solution)/shard_map/jit(cholesky)/cholesky | solution.py:29
  298.9 11.7 %cholesky.493 = f32[128,128]{1,0:T(8,128)S(1)} custom-call(f32[128,128]{1,0:T(8,128)S(1)} %cholesky.676), custom_call_target="Cholesky" | custom-call | tf_op jit(solution)/shard_map/jit(cholesky)/cholesky | solution.py:29
  311.4 9.8 %custom-call.66 = f32[1,128,128]{1,2,0:T(8,128)S(1)} custom-call(f32[1,128,128]{2,1,0:T(8,128)S(1)} %get-tuple-element.13), custom_call_target="InvertDiagBlocksLowerTriangular" | custom-call | tf_op jit(solution)/shard_map/jit(cholesky)/cholesky | solution.py:29
  325.8 11.7 %cholesky.512 = f32[128,128]{1,0:T(8,128)S(1)} custom-call(f32[128,128]{1,0:T(8,128)S(1)} %cholesky.681), custom_call_target="Cholesky" | custom-call | tf_op jit(solution)/shard_map/jit(cholesky)/cholesky | solution.py:29
  338.3 9.8 %custom-call.67 = f32[1,128,128]{1,2,0:T(8,128)S(1)} custom-call(f32[1,128,128]{2,1,0:T(8,128)S(1)} %get-tuple-element.11), custom_call_target="InvertDiagBlocksLowerTriangular" | custom-call | tf_op jit(solution)/shard_map/jit(cholesky)/cholesky | solution.py:29
  352.4 12.1 %cholesky.531 = f32[128,128]{1,0:T(8,128)S(1)} custom-call(f32[128,128]{1,0:T(8,128)S(1)} %cholesky.686), custom_call_target="Cholesky" | custom-call | tf_op jit(solution)/shard_map/jit(cholesky)/cholesky | solution.py:29
  365.3 9.8 %custom-call.68 = f32[1,128,128]{1,2,0:T(8,128)S(1)} custom-call(f32[1,128,128]{2,1,0:T(8,128)S(1)} %get-tuple-element.9), custom_call_target="InvertDiagBlocksLowerTriangular" | custom-call | tf_op jit(solution)/shard_map/jit(cholesky)/cholesky | solution.py:29
  379.4 11.7 %cholesky.551 = f32[128,128]{1,0:T(8,128)S(1)} custom-call(f32[128,128]{1,0:T(8,128)S(1)} %cholesky.691), custom_call_target="Cholesky" | custom-call | tf_op jit(solution)/shard_map/jit(cholesky)/cholesky | solution.py:29
  391.9 9.8 %custom-call.69 = f32[1,128,128]{1,2,0:T(8,128)S(1)} custom-call(f32[1,128,128]{2,1,0:T(8,128)S(1)} %get-tuple-element.7), custom_call_target="InvertDiagBlocksLowerTriangular" | custom-call | tf_op jit(solution)/shard_map/jit(cholesky)/cholesky | solution.py:29
  405.5 11.7 %cholesky.571 = f32[128,128]{1,0:T(8,128)S(1)} custom-call(f32[128,128]{1,0:T(8,128)S(1)} %cholesky.696), custom_call_target="Cholesky" | custom-call | tf_op jit(solution)/shard_map/jit(cholesky)/cholesky | solution.py:29
  418.0 9.8 %custom-call.70 = f32[1,128,128]{1,2,0:T(8,128)S(1)} custom-call(f32[1,128,128]{2,1,0:T(8,128)S(1)} %get-tuple-element.5), custom_call_target="InvertDiagBlocksLowerTriangular" | custom-call | tf_op jit(solution)/shard_map/jit(cholesky)/cholesky | solution.py:29
  430.9 11.7 %cholesky.589 = f32[128,128]{1,0:T(8,128)S(1)} custom-call(f32[128,128]{1,0:T(8,128)S(1)} %convolution_subtract_fusion.6), custom_call_target="Cholesky" | custom-call | tf_op jit(solution)/shard_map/jit(cholesky)/cholesky | solution.py:29
  442.7 9.0 %fusion.78 = f32[1024,128]{1,0:T(8,128)S(1)} fusion(f32[1024,128]{1,0:T(8,128)S(1)} %copy-done, f32[1024,1024]{0,1:T(8,128)} %all-reduce.3.cloned.1.call-done), kind=kOutput, calls=%fused_computation.137 | convolution fusion | flops 1614807040 | bytes 5242880 | tf_op jit(solution)/shard_map/dot_general | solution.py:32
  452.9 11.7 %cholesky.636 = f32[128,128]{1,0:T(8,128)S(1)} custom-call(f32[128,128]{1,0:T(8,128)S(1)} %fusion.38), custom_call_target="Cholesky" | custom-call | tf_op jit(solution)/shard_map/jit(cholesky)/cholesky | solution.py:42
  465.9 9.8 %custom-call.73 = f32[1,128,128]{1,2,0:T(8,128)S(1)} custom-call(f32[1,128,128]{2,1,0:T(8,128)S(1)} %fusion.21), custom_call_target="InvertDiagBlocksLowerTriangular" | custom-call | tf_op jit(solution)/shard_map/triangular_solve/custom-call.16 | solution.py:43
  476.4 9.2 %fusion.77 = f32[1024,128]{1,0:T(8,128)S(1)} fusion(f32[1024,128]{0,1:T(8,128)S(1)} %convolution_bitcast_fusion.2, f32[1024,1024]{0,1:T(8,128)} %all-reduce.3.cloned.1.call-done), kind=kOutput, calls=%fused_computation.136 | convolution fusion | flops 1614807040 | bytes 5242880 | tf_op jit(solution)/shard_map/dot_general | solution.py:32
  486.7 11.7 %cholesky.647 = f32[128,128]{1,0:T(8,128)S(1)} custom-call(f32[128,128]{1,0:T(8,128)S(1)} %fusion.36), custom_call_target="Cholesky" | custom-call | tf_op jit(solution)/shard_map/jit(cholesky)/cholesky | solution.py:42
  499.8 9.8 %custom-call.74 = f32[1,128,128]{1,2,0:T(8,128)S(1)} custom-call(f32[1,128,128]{2,1,0:T(8,128)S(1)} %fusion.22), custom_call_target="InvertDiagBlocksLowerTriangular" | custom-call | tf_op jit(solution)/shard_map/triangular_solve/custom-call.16 | solution.py:43
  510.3 9.0 %fusion.76 = f32[1024,128]{1,0:T(8,128)S(1)} fusion(f32[1024,128]{0,1:T(8,128)S(1)} %convolution_bitcast_fusion.1, f32[1024,1024]{0,1:T(8,128)} %all-reduce.3.cloned.1.call-done), kind=kOutput, calls=%fused_computation.135 | convolution fusion | flops 1614807040 | bytes 5242880 | tf_op jit(solution)/shard_map/dot_general | solution.py:32
  520.3 11.7 %cholesky.658 = f32[128,128]{1,0:T(8,128)S(1)} custom-call(f32[128,128]{1,0:T(8,128)S(1)} %fusion.34), custom_call_target="Cholesky" | custom-call | tf_op jit(solution)/shard_map/jit(cholesky)/cholesky | solution.py:42
  533.4 9.8 %custom-call.75 = f32[1,128,128]{1,2,0:T(8,128)S(1)} custom-call(f32[1,128,128]{2,1,0:T(8,128)S(1)} %fusion.23), custom_call_target="InvertDiagBlocksLowerTriangular" | custom-call | tf_op jit(solution)/shard_map/triangular_solve/custom-call.16 | solution.py:43
  553.9 4.9 select_bitcast_fusion
  558.8 4.2 fusion.1
  (89 shorter events, 53.5 us)
Async XLA Ops:
  7.2 435.6 %copy-start = (f32[1024,128]{1,0:T(8,128)S(1)}, f32[1024,128]{1,0:T(8,128)}, u32[]{:S(2)}) copy-start(f32[1024,128]{1,0:T(8,128)} %param.8) | copy-start | bytes 1572868
  7.2 93.9 %all-gather.2.cloned.1.call-start = ((), (), s32[]{:S(2)}) async-start(), calls=%async_computation | async-start | bytes 10485760 | tf_op jit(solution)/shard_map/all_gather | solution.py:20
  11.1 218.1 %all-reduce.3.cloned.1.call-start = ((), (), s32[]{:S(2)}) async-start(), calls=%async_computation.1 | async-start | bytes 8388608 | tf_op jit(solution)/shard_map/psum | solution.py:26
  244.6 2.0 copy-start.2
  294.5 2.0 copy-start.1
Sparse Core Ops, SparseCore 0:
  11.2 89.7 all-gather.1
  116.2 112.9 all-reduce.2
where the time goes:
time: 575 us; the launch traced here: 570 us
  other arithmetic  254 us (44%)
  waiting for transfers between devices  203 us (35%)
  matrix products  77.3 us (13%)
  between operations  19.6 us (3%)
  local copies, waits for them, and re-layouts  15.6 us (3%)
    another operation x30, other arithmetic, body(): upper_factor = jnp.linalg.cholesky(shifted).T  167 us
    psum x1, waiting for transfers between devices, body(): gram_sum = lax.psum(partial_gram, 'dof')  113 us
    all_gather x1, waiting for transfers between devices, body(): gathered_slab = lax.all_gather(masked, 'snap', axis=1, tiled=True)  89.9 us
    another operation x9, other arithmetic, body(): lower_factor = jnp.linalg.cholesky(correlation)  37.2 us
    another operation x6, other arithmetic, body(): lax.linalg.triangular_solve(lower_factor, image, left_side=False, lower=T...  31.4 us
    dot_general x3, matrix products, body(): jnp.dot(shifted, subspace, precision=lax.Precision.HIGHEST, preferred_ele...  27.2 us
    another operation x14, matrix products, body(): upper_factor = jnp.linalg.cholesky(shifted).T  25.9 us
    dot_general x1, matrix products, body(): lax.dot_general(gathered_slab, gathered_slab, contract, preferred_element...  15 us
  transfers between devices with their start and end apart: 2, of which 2 were waited for; matrix products, arithmetic and copies ran while one was open for 0% of the time, Pallas kernels for 0%

commit v1 on v0

--- a/solution.py
+++ b/solution.py
@@ -6,6 +6,14 @@
 STEPS = 64
 ITERS = 3
 PASSES = 16
+
+
+def tiled_gather(array, axis, dim):
+    count = lax.axis_size(axis)
+    repeats = [count if d == dim else 1 for d in range(array.ndim)]
+    return lax.all_to_all(
+        jnp.tile(array, repeats), axis, split_axis=dim, concat_axis=dim, tiled=True
+    )
 
 
 def body(snapshots, lengths, start_block):
@@ -17,7 +25,7 @@
     col_length = jnp.sum(jnp.where(lookup, lengths[None, :], 0), axis=1)
     active = columns % STEPS < col_length
     masked = jnp.where(active[None, :], snapshots, jnp.zeros_like(snapshots))
-    gathered_slab = lax.all_gather(masked, "snap", axis=1, tiled=True)
+    gathered_slab = tiled_gather(masked, "snap", 1)
     row_count = gathered_slab.shape[0] * lax.axis_size("dof")
     contract = (((0,), (0,)), ((), ()))
     partial_gram = lax.dot_general(

time: 575 us -> 596 us (1.037)
  blocking collectives: 0 us -> 97.8 us
  waiting for transfers between devices: 203 us -> 114 us
  local copies, waits for them, and re-layouts: 15.6 us -> 27.5 us
    all_to_all x0 -> x1, blocking collectives: none -> 97.8 us  [tiled_gather(): lax.all_to_all(jnp.tile(array, repeats), axis, split_axis=dim, concat_axi...]
    all_gather x1 -> x0, waiting for transfers between devices: 89.9 us -> none  [body(): gathered_slab = lax.all_gather(masked, 'snap', axis=1, tiled=True)]
    all_to_all x0 -> x1, local copies, waits for them, and re-layouts: none -> 11.3 us  [tiled_gather(): lax.all_to_all(jnp.tile(array, repeats), axis, split_axis=dim, concat_axi...]
  transfers between devices with their start and end apart: 2 -> 1, of which waited for: 2 -> 1; matrix products, arithmetic and copies ran while one was open for 0% -> 0% of each run, Pallas kernels for 0% -> 0%
where the time goes in v1:
time: 596 us; the launch traced here: 590 us
  other arithmetic  253 us (42%)
  waiting for transfers between devices  114 us (19%)
  blocking collectives  97.8 us (16%)
  matrix products  78.7 us (13%)
  local copies, waits for them, and re-layouts  27.5 us (5%)
  between operations  19.6 us (3%)
    another operation x30, other arithmetic, body(): upper_factor = jnp.linalg.cholesky(shifted).T  168 us
    psum x1, waiting for transfers between devices, body(): gram_sum = lax.psum(partial_gram, 'dof')  114 us
    all_to_all x1, blocking collectives, tiled_gather(): lax.all_to_all(jnp.tile(array, repeats), axis, split_axis=dim, concat_axi...  97.8 us
    another operation x9, other arithmetic, body(): lower_factor = jnp.linalg.cholesky(correlation)  37.2 us
    another operation x6, other arithmetic, body(): lax.linalg.triangular_solve(lower_factor, image, left_side=False, lower=T...  31.4 us
    dot_general x3, matrix products, body(): jnp.dot(shifted, subspace, precision=lax.Precision.HIGHEST, preferred_ele...  27.2 us
    another operation x14, matrix products, body(): upper_factor = jnp.linalg.cholesky(shifted).T  25.9 us
    dot_general x1, matrix products, body(): lax.dot_general(gathered_slab, gathered_slab, contract, preferred_element...  15.9 us
  transfers between devices with their start and end apart: 1, of which 1 were waited for; matrix products, arithmetic and copies ran while one was open for 0% of the time, Pallas kernels for 0%

profile of v1, /device:TPU:1, one launch (start us, length us, event | category | flops | bytes accessed | tf_op | source)
XLA Modules:
  0.0 590.2 jit_solution(10818100573725221655)
XLA Ops:
  10.3 97.8 %all_to_all.9 = bf16[4096,4,256]{2,0,1:T(8,128)(2,1)} all-to-all(bf16[4096,4,256]{2,0,1:T(8,128)(2,1)S(1)} %tile.2), channel_id=1, replica_groups=mesh['dof'=32,'snap'=4] {'snap'}, dimensions={1} | all-to-all | bytes 16777216 | tf_op jit(solution)/shard_map/all_to_all | solution.py:14
  108.1 11.3 %copy.66 = bf16[4096,4,256]{0,2,1:T(8,128)(2,1)} copy(bf16[4096,4,256]{2,0,1:T(8,128)(2,1)} %all_to_all.9) | data formatting | bytes 16777216 | tf_op jit(solution)/shard_map/all_to_all | solution.py:14
  119.4 15.9 %fusion.79 = f32[1024,1024]{0,1:T(8,128)} fusion(bf16[4096,1024]{0,1:T(8,128)(2,1)} %bitcast.91), kind=kOutput, calls=%fused_computation.138 | convolution fusion | flops 8589934592 | bytes 12582912 | tf_op jit(solution)/shard_map/dot_general | solution.py:31
  135.4 113.5 %all-reduce.3.cloned.1.call-done = f32[1024,1024]{0,1:T(8,128)} async-done(((f32[1024,1024]{0,1:T(8,128)}), f32[1024,1024]{0,1:T(8,128)}) %all-reduce.3.cloned.1.call-update) | async-done | bytes 4194320 | tf_op jit(solution)/shard_map/psum | solution.py:34
  248.9 5.1 select_add_fusion
  253.9 5.8 copy.71
  266.3 11.7 %cholesky.247 = f32[128,128]{1,0:T(8,128)S(1)} custom-call(f32[128,128]{1,0:T(8,128)S(1)} %cholesky.667), custom_call_target="Cholesky" | custom-call | tf_op jit(solution)/shard_map/jit(cholesky)/cholesky | solution.py:37
  278.1 9.8 %custom-call.64 = f32[1,128,128]{1,2,0:T(8,128)S(1)} custom-call(f32[1,128,128]{2,1,0:T(8,128)S(1)} %get-tuple-element.17), custom_call_target="InvertDiagBlocksLowerTriangular" | custom-call | tf_op jit(solution)/shard_map/jit(cholesky)/cholesky | solution.py:37
  291.2 11.7 %cholesky.270 = f32[128,128]{1,0:T(8,128)S(1)} custom-call(f32[128,128]{1,0:T(8,128)S(1)} %cholesky.671), custom_call_target="Cholesky" | custom-call | tf_op jit(solution)/shard_map/jit(cholesky)/cholesky | solution.py:37
  303.2 9.8 %custom-call.65 = f32[1,128,128]{1,2,0:T(8,128)S(1)} custom-call(f32[1,128,128]{2,1,0:T(8,128)S(1)} %get-tuple-element.15), custom_call_target="InvertDiagBlocksLowerTriangular" | custom-call | tf_op jit(solution)/shard_map/jit(cholesky)/cholesky | solution.py:37
  318.6 11.7 %cholesky.493 = f32[128,128]{1,0:T(8,128)S(1)} custom-call(f32[128,128]{1,0:T(8,128)S(1)} %cholesky.676), custom_call_target="Cholesky" | custom-call | tf_op jit(solution)/shard_map/jit(cholesky)/cholesky | solution.py:37
  331.1 9.8 %custom-call.66 = f32[1,128,128]{1,2,0:T(8,128)S(1)} custom-call(f32[1,128,128]{2,1,0:T(8,128)S(1)} %get-tuple-element.13), custom_call_target="InvertDiagBlocksLowerTriangular" | custom-call | tf_op jit(solution)/shard_map/jit(cholesky)/cholesky | solution.py:37
  345.4 11.7 %cholesky.512 = f32[128,128]{1,0:T(8,128)S(1)} custom-call(f32[128,128]{1,0:T(8,128)S(1)} %cholesky.681), custom_call_target="Cholesky" | custom-call | tf_op jit(solution)/shard_map/jit(cholesky)/cholesky | solution.py:37
  357.9 9.8 %custom-call.67 = f32[1,128,128]{1,2,0:T(8,128)S(1)} custom-call(f32[1,128,128]{2,1,0:T(8,128)S(1)} %get-tuple-element.11), custom_call_target="InvertDiagBlocksLowerTriangular" | custom-call | tf_op jit(solution)/shard_map/jit(cholesky)/cholesky | solution.py:37
  372.1 12.1 %cholesky.531 = f32[128,128]{1,0:T(8,128)S(1)} custom-call(f32[128,128]{1,0:T(8,128)S(1)} %cholesky.686), custom_call_target="Cholesky" | custom-call | tf_op jit(solution)/shard_map/jit(cholesky)/cholesky | solution.py:37
  384.9 9.8 %custom-call.68 = f32[1,128,128]{1,2,0:T(8,128)S(1)} custom-call(f32[1,128,128]{2,1,0:T(8,128)S(1)} %get-tuple-element.9), custom_call_target="InvertDiagBlocksLowerTriangular" | custom-call | tf_op jit(solution)/shard_map/jit(cholesky)/cholesky | solution.py:37
  399.0 11.7 %cholesky.551 = f32[128,128]{1,0:T(8,128)S(1)} custom-call(f32[128,128]{1,0:T(8,128)S(1)} %cholesky.691), custom_call_target="Cholesky" | custom-call | tf_op jit(solution)/shard_map/jit(cholesky)/cholesky | solution.py:37
  411.5 9.8 %custom-call.69 = f32[1,128,128]{1,2,0:T(8,128)S(1)} custom-call(f32[1,128,128]{2,1,0:T(8,128)S(1)} %get-tuple-element.7), custom_call_target="InvertDiagBlocksLowerTriangular" | custom-call | tf_op jit(solution)/shard_map/jit(cholesky)/cholesky | solution.py:37
  425.1 11.7 %cholesky.571 = f32[128,128]{1,0:T(8,128)S(1)} custom-call(f32[128,128]{1,0:T(8,128)S(1)} %cholesky.696), custom_call_target="Cholesky" | custom-call | tf_op jit(solution)/shard_map/jit(cholesky)/cholesky | solution.py:37
  437.6 9.8 %custom-call.70 = f32[1,128,128]{1,2,0:T(8,128)S(1)} custom-call(f32[1,128,128]{2,1,0:T(8,128)S(1)} %get-tuple-element.5), custom_call_target="InvertDiagBlocksLowerTriangular" | custom-call | tf_op jit(solution)/shard_map/jit(cholesky)/cholesky | solution.py:37
  450.5 11.7 %cholesky.589 = f32[128,128]{1,0:T(8,128)S(1)} custom-call(f32[128,128]{1,0:T(8,128)S(1)} %convolution_subtract_fusion.6), custom_call_target="Cholesky" | custom-call | tf_op jit(solution)/shard_map/jit(cholesky)/cholesky | solution.py:37
  462.4 9.0 %fusion.78 = f32[1024,128]{1,0:T(8,128)S(1)} fusion(f32[1024,128]{1,0:T(8,128)S(1)} %copy-done, f32[1024,1024]{0,1:T(8,128)} %all-reduce.3.cloned.1.call-done), kind=kOutput, calls=%fused_computation.137 | convolution fusion | flops 1614807040 | bytes 5242880 | tf_op jit(solution)/shard_map/dot_general | solution.py:40
  472.5 11.7 %cholesky.636 = f32[128,128]{1,0:T(8,128)S(1)} custom-call(f32[128,128]{1,0:T(8,128)S(1)} %fusion.38), custom_call_target="Cholesky" | custom-call | tf_op jit(solution)/shard_map/jit(cholesky)/cholesky | solution.py:50
  485.5 9.8 %custom-call.73 = f32[1,128,128]{1,2,0:T(8,128)S(1)} custom-call(f32[1,128,128]{2,1,0:T(8,128)S(1)} %fusion.21), custom_call_target="InvertDiagBlocksLowerTriangular" | custom-call | tf_op jit(solution)/shard_map/triangular_solve/custom-call.16 | solution.py:51
  496.0 9.2 %fusion.77 = f32[1024,128]{1,0:T(8,128)S(1)} fusion(f32[1024,128]{0,1:T(8,128)S(1)} %convolution_bitcast_fusion.2, f32[1024,1024]{0,1:T(8,128)} %all-reduce.3.cloned.1.call-done), kind=kOutput, calls=%fused_computation.136 | convolution fusion | flops 1614807040 | bytes 5242880 | tf_op jit(solution)/shard_map/dot_general | solution.py:40
  506.4 11.7 %cholesky.647 = f32[128,128]{1,0:T(8,128)S(1)} custom-call(f32[128,128]{1,0:T(8,128)S(1)} %fusion.36), custom_call_target="Cholesky" | custom-call | tf_op jit(solution)/shard_map/jit(cholesky)/cholesky | solution.py:50
  519.4 9.8 %custom-call.74 = f32[1,128,128]{1,2,0:T(8,128)S(1)} custom-call(f32[1,128,128]{2,1,0:T(8,128)S(1)} %fusion.22), custom_call_target="InvertDiagBlocksLowerTriangular" | custom-call | tf_op jit(solution)/shard_map/triangular_solve/custom-call.16 | solution.py:51
  529.9 9.0 %fusion.76 = f32[1024,128]{1,0:T(8,128)S(1)} fusion(f32[1024,128]{0,1:T(8,128)S(1)} %convolution_bitcast_fusion.1, f32[1024,1024]{0,1:T(8,128)} %all-reduce.3.cloned.1.call-done), kind=kOutput, calls=%fused_computation.135 | convolution fusion | flops 1614807040 | bytes 5242880 | tf_op jit(solution)/shard_map/dot_general | solution.py:40
  540.0 11.7 %cholesky.658 = f32[128,128]{1,0:T(8,128)S(1)} custom-call(f32[128,128]{1,0:T(8,128)S(1)} %fusion.34), custom_call_target="Cholesky" | custom-call | tf_op jit(solution)/shard_map/jit(cholesky)/cholesky | solution.py:50
  553.0 9.8 %custom-call.75 = f32[1,128,128]{1,2,0:T(8,128)S(1)} custom-call(f32[1,128,128]{2,1,0:T(8,128)S(1)} %fusion.23), custom_call_target="InvertDiagBlocksLowerTriangular" | custom-call | tf_op jit(solution)/shard_map/triangular_solve/custom-call.16 | solution.py:51
  568.0 4.7 fusion.1
  578.2 4.9 select_bitcast_fusion
  (89 shorter events, 57.2 us)
Async XLA Ops:
  7.2 455.2 %copy-start = (f32[1024,128]{1,0:T(8,128)S(1)}, f32[1024,128]{1,0:T(8,128)}, u32[]{:S(2)}) copy-start(f32[1024,128]{1,0:T(8,128)} %param.8) | copy-start | bytes 1572868
  7.2 241.7 %all-reduce.3.cloned.1.call-start = ((), (), s32[]{:S(2)}) async-start(), calls=%async_computation.1 | async-start | bytes 8388608 | tf_op jit(solution)/shard_map/psum | solution.py:34
  264.2 2.0 copy-start.2
  314.2 2.0 copy-start.1
Sparse Core Ops, SparseCore 0:
  135.5 113.3 all-reduce.2
